TPU v7x, 512 devices: a whole 4x4x16 slice. The times are simulated.
512 devices in a mesh: seq: 32 (over y, z_hi, core), chan: 16 (over x, z_lo).
Axes of the slice: x: 4, y: 4, z: 16 (z_hi: 4, z_lo: 4; z = z_hi * 4 + z_lo), core: 2. Of those that a mesh axis runs over, the one named last changes fastest.
Arguments:
- streams: bfloat16 [5, 8192, 8192], P(None, 'seq', 'chan'), may hold values from -6 to 6
- short_filter: bfloat16 [7, 8192], P(None, 'chan'), may hold values from -2 to 2
- long_filter: bfloat16 [128, 8192], P(None, 'chan'), may hold values from -0.5 to 0.5
- edit_table: bfloat16 [64, 8, 8192], P('seq', None, 'chan'), may hold values from -0.25 to 0.25
- edit_bias: float32 [64, 4], replicated, may hold values from -8 to 8
- seq_tiles: int32 [4], replicated, may hold values from 1 to 32, 64 in all
- seq_tenant: int32 [4], replicated, may hold values from 0 to 63
Outputs:
- edited: bfloat16 [8192, 8192], P('seq', 'chan')
Inputs may be any that keep to these rules, and one draw needn't show every extreme that they name: `seq_tiles`: each sequence fills whole tiles; the sequences fill all 64 tiles in order and the longest has 32.
All inputs are finite; a program needn't handle non-finite values.
Results may differ from a plain program's by a relative error of at most 0.013.
Values may be sent and summed in bfloat16 or wider, within the bound.
No kernel may reach another device: no remote copies, remote signals or barrier semaphores. Data moves between devices by JAX's collectives and lax.ppermute only.
A program may use at most 64 MiB of HBM per device.

v0:
```python
import jax
import jax.numpy as jnp
from jax import lax
from jax.sharding import PartitionSpec as P

TILE_ROWS = 128
SEQS = 4


def from_behind(block, axis, distance):
    devices = range(lax.axis_size(axis))
    route = [(i - distance, i) for i in devices if i - distance in devices]
    return lax.ppermute(block, axis, route)


def depth_conv(window, taps_filter):
    width = window.shape[-1]
    kernel = taps_filter[::-1][:, None, :]
    return lax.conv_general_dilated(
        window,
        kernel,
        (1,),
        "VALID",
        dimension_numbers=("NWC", "WIO", "NWC"),
        feature_group_count=width,
        preferred_element_type=jnp.float32,
    )


def tiled_conv(field, border, starts, taps_filter):
    rows_here, width = field.shape
    reach = taps_filter.shape[0]
    tile_count = rows_here // TILE_ROWS
    tiles = field.reshape(tile_count, TILE_ROWS, width)
    trailing = tiles[:, TILE_ROWS - (reach - 1) :, :]
    earlier = jnp.concatenate([border[None], trailing[:-1]], axis=0)
    earlier = jnp.where(starts[:, None, None], jnp.zeros_like(earlier), earlier)
    window = jnp.concatenate([earlier, tiles], axis=1)
    return depth_conv(window, taps_filter).reshape(rows_here, width)


def on_device(streams, short_filter, long_filter, edit_table, edit_bias, seq_tiles, seq_tenant):
    rows_here = streams.shape[1]
    width = streams.shape[2]
    short_reach = short_filter.shape[0]
    long_reach = long_filter.shape[0]
    tile_count = rows_here // TILE_ROWS
    seq_ends = jnp.cumsum(seq_tiles)
    first_tile = lax.axis_index("seq") * tile_count
    tile_ids = first_tile + jnp.arange(tile_count, dtype=jnp.int32)
    seq_of = jnp.sum((seq_ends[None, :] <= tile_ids[:, None]).astype(jnp.int32), axis=1)
    starts = (tile_ids == 0) | jnp.any(seq_ends[None, :] == tile_ids[:, None], axis=1)
    first_gate = streams[0]
    first_key = streams[1]
    second_gate = streams[3]
    second_key = streams[4]
    gated = (first_key.astype(jnp.float32) * streams[2].astype(jnp.float32)).astype(jnp.bfloat16)
    short_border = from_behind(gated[rows_here - (short_reach - 1) :], "seq", 1)
    short_out = tiled_conv(gated, short_border, starts, short_filter)
    mixed = (first_gate.astype(jnp.float32) * short_out).astype(jnp.bfloat16)
    carried = (second_key.astype(jnp.float32) * mixed.astype(jnp.float32)).astype(jnp.bfloat16)
    long_border = from_behind(carried[rows_here - (long_reach - 1) :], "seq", 1)
    long_out = tiled_conv(carried, long_border, starts, long_filter)
    hidden = (second_gate.astype(jnp.float32) * long_out).astype(jnp.bfloat16)
    rows_per = edit_table.shape[1]
    rank = rows_per // 2
    all_rows = lax.all_gather(edit_table, "seq", axis=0, tiled=True)
    tenant_count = all_rows.shape[0]
    picker = (seq_tenant[:, None] == jnp.arange(tenant_count, dtype=jnp.int32)[None, :]).astype(
        jnp.bfloat16
    )
    chosen = jnp.dot(
        picker, all_rows.reshape(tenant_count, rows_per * width), preferred_element_type=jnp.float32
    )
    chosen = chosen.astype(jnp.bfloat16).reshape(SEQS, rows_per, width)
    tok_seq = jnp.repeat(seq_of, TILE_ROWS)
    seq_onehot = (tok_seq[:, None] == jnp.arange(SEQS, dtype=jnp.int32)[None, :]).astype(
        jnp.float32
    )
    projected = jnp.dot(
        hidden, chosen.reshape(SEQS * rows_per, width).T, preferred_element_type=jnp.float32
    )
    projected = projected.reshape(rows_here, SEQS, rows_per)
    selected = jnp.sum(projected * seq_onehot[:, :, None], axis=1)
    summed = lax.psum(selected, "chan")
    tenant_total = edit_bias.shape[0]
    bias_pick = (seq_tenant[:, None] == jnp.arange(tenant_total, dtype=jnp.int32)[None, :]).astype(
        jnp.float32
    )
    bias_seq = jnp.dot(bias_pick, edit_bias, precision=lax.Precision.HIGHEST)
    bias_tok = jnp.dot(seq_onehot, bias_seq, precision=lax.Precision.HIGHEST)
    coefficient = summed[:, rank:] - summed[:, :rank] + bias_tok
    spread = (seq_onehot[:, :, None] * coefficient[:, None, :]).reshape(rows_here, SEQS * rank)
    rows_r = chosen[:, :rank, :].reshape(SEQS * rank, width).astype(jnp.float32)
    change = jnp.dot(spread, rows_r, precision=lax.Precision.HIGHEST)
    return (hidden.astype(jnp.float32) + change).astype(jnp.bfloat16)


def solution(mesh):
    in_specs = (
        P(None, "seq", "chan"),
        P(None, "chan"),
        P(None, "chan"),
        P("seq", None, "chan"),
        P(),
        P(),
        P(),
    )
    out_specs = P("seq", "chan")
    return jax.shard_map(
        on_device, mesh=mesh, in_specs=in_specs, out_specs=out_specs, check_vma=False
    )
```

profile of v0, /device:TPU:8, one launch (start us, length us, event | category | flops | bytes accessed | tf_op | source)
XLA Modules:
  0.0 135.5 jit_solution(4230756904072077659)
XLA Ops:
  0.0 1.1 multiply_convert_fusion.3
  1.1 1.9 %collective-permute-start = (bf16[6,512]{1,0:T(8,128)(2,1)S(1)}, bf16[6,512]{1,0:T(8,128)(2,1)S(1)}, u32[]{:S(2)}, u32[]{:S(2)}) collective-permute-start(bf16[6,512]{1,0:T(8,128)(2,1)S(1)} %slice_bitcast_fusion), channel_id=1, source_target_pairs={{0,16},{16,32},{32,48},{48,64},{64,80},{80,96},{96,112},{112,128},... | collective-permute-start | bytes 18440 | tf_op jit(solution)/shard_map/ppermute | solution.py:13
  3.1 2.2 %slice_convert_fusion.2 = (f32[1,256,512]{2,1,0:T(8,128)S(1)}, f32[256,512]{1,0:T(8,128)S(1)}, f32[256,512]{1,0:T(8,128)}, f32[1,256,512]{2,1,0:T(8,128)S(1)}, f32[1,256,512]{2,1,0:T(8,128)S(1)}) fusion(bf16[5,256,512]{2,1,0:T(8,128)(2,1)} %param.7), kind=kLoop, calls=%fused_computation.30 | loop fusion | flops 393216 | bytes 3407872 | tf_op jit(solution)/shard_map/convert_element_type | solution.py:64
  5.3 0.2 reduce-window.8
  5.5 0.2 compare_reduce_fusion
  5.7 0.2 fusion.22
  6.0 56.8 %all_gather.3 = bf16[64,8,512]{2,1,0:T(8,128)(2,1)S(1)} all-gather(bf16[2,8,512]{2,1,0:T(8,128)(2,1)S(1)} %copy-done.4), channel_id=1, replica_groups=mesh['seq'=32,'chan'=16] {'seq'}, dimensions={0}, use_global_device_ids=true | all-gather | bytes 540672 | tf_op jit(solution)/shard_map/all_gather | solution.py:67
  62.9 0.2 convolution_convert_fusion
  63.3 1.3 rev.7
  64.8 0.2 copy.72
  65.1 0.2 pad.clone
  65.4 0.3 fusion.6
  65.7 0.3 convolution_select_fusion
  66.0 0.3 copy.67
  66.6 0.9 copy-done.1
  67.6 2.3 %collective-permute-start.1 = (bf16[127,512]{1,0:T(8,128)(2,1)S(1)}, bf16[127,512]{1,0:T(8,128)(2,1)S(1)}, u32[]{:S(2)}, u32[]{:S(2)}) collective-permute-start(bf16[127,512]{1,0:T(8,128)(2,1)S(1)} %fusion.9), channel_id=1, source_target_pairs={{0,16},{16,32},{32,48},{48,64},{64,80},{80,96},{96,112},{112,128},... | collective-permute-start | bytes 390152 | tf_op jit(solution)/shard_map/ppermute | solution.py:13
  69.9 0.2 fusion.20
  70.1 10.8 %collective-permute-done.1 = bf16[127,512]{1,0:T(8,128)(2,1)S(1)} collective-permute-done((bf16[127,512]{1,0:T(8,128)(2,1)S(1)}, bf16[127,512]{1,0:T(8,128)(2,1)S(1)}, u32[]{:S(2)}, u32[]{:S(2)}) %collective-permute-start.1) | collective-permute-done | bytes 130080 | tf_op jit(solution)/shard_map/ppermute | solution.py:13
  81.1 6.7 %fusion.4 = f32[2,128,512]{2,0,1:T(2,128)S(1)} fusion(bf16[2,255,512]{2,1,0:T(8,128)(2,1)S(1)} %pad_maximum_fusion, bf16[128,1,512]{2,0,1:T(8,128)(2,1)S(1)} %bitcast.63), kind=kOutput, calls=%fused_computation.16 | convolution fusion | flops 33554432 | bytes 1177600 | tf_op jit(solution)/shard_map/conv_general_dilated | solution.py:19
  88.0 0.2 fusion.2
  88.2 45.0 %psum.7 = f32[256,8]{0,1:T(8,128)S(1)} all-reduce(f32[256,8]{0,1:T(8,128)S(1)} %fusion.2), channel_id=1, replica_groups=mesh['seq'=32,'chan'=16] {'chan'}, use_global_device_ids=true, to_apply=%region_4.5 | all-reduce | flops 2048 | bytes 16384 | tf_op jit(solution)/shard_map/psum | solution.py:85
  133.1 1.0 fusion.3
  134.1 0.2 convolution_add_fusion
  134.3 1.2 fusion.1
  (37 shorter events, 1.4 us)
Async XLA Ops:
  0.0 69.9 %copy-start = (f32[64,4]{0,1:T(4,128)S(1)}, f32[64,4]{0,1:T(4,128)}, u32[]{:S(2)}) copy-start(f32[64,4]{0,1:T(4,128)} %param.11) | copy-start | bytes 3076
  1.1 63.6 %collective-permute-start = (bf16[6,512]{1,0:T(8,128)(2,1)S(1)}, bf16[6,512]{1,0:T(8,128)(2,1)S(1)}, u32[]{:S(2)}, u32[]{:S(2)}) collective-permute-start(bf16[6,512]{1,0:T(8,128)(2,1)S(1)} %slice_bitcast_fusion), channel_id=1, source_target_pairs={{0,16},{16,32},{32,48},{48,64},{64,80},{80,96},{96,112},{112,128},... | collective-permute-start | bytes 18440 | tf_op jit(solution)/shard_map/ppermute | solution.py:13
  3.1 2.3 %copy-start.7 = (s32[4]{0:T(128)S(1)}, s32[4]{0:T(128)}, u32[]{:S(2)}) copy-start(s32[4]{0:T(128)} %param.12) | copy-start | bytes 52
  3.1 2.9 %copy-start.4 = (bf16[2,8,512]{2,1,0:T(8,128)(2,1)S(1)}, bf16[2,8,512]{2,1,0:T(8,128)(2,1)}, u32[]{:S(2)}) copy-start(bf16[2,8,512]{2,1,0:T(8,128)(2,1)} %param.10) | copy-start | bytes 49156
  5.3 57.6 %copy-start.6 = (s32[4]{0:T(128)S(1)}, s32[4]{0:T(128)}, u32[]{:S(2)}) copy-start(s32[4]{0:T(128)} %param.13) | copy-start | bytes 52
  5.3 57.9 %copy-start.5 = (bf16[7,512]{1,0:T(8,128)(2,1)S(1)}, bf16[7,512]{1,0:T(8,128)(2,1)}, u32[]{:S(2)}) copy-start(bf16[7,512]{1,0:T(8,128)(2,1)} %param.8) | copy-start | bytes 21508
  5.3 58.0 %copy-start.2 = (bf16[128,512]{1,0:T(8,128)(2,1)S(1)}, bf16[128,512]{1,0:T(8,128)(2,1)}, u32[]{:S(2)}) copy-start(bf16[128,512]{1,0:T(8,128)(2,1)} %param.9) | copy-start | bytes 393220
  64.7 1.0 copy-start.8
  66.5 1.0 copy-start.1
  67.5 13.6 %copy-start.3 = (bf16[128,512]{1,0:T(8,128)(2,1)S(1)}, bf16[128,512]{1,0:T(8,128)(2,1)}, u32[]{:S(2)}) copy-start(bf16[128,512]{1,0:T(8,128)(2,1)} %rev.7) | copy-start | bytes 393220
  67.6 13.3 %collective-permute-start.1 = (bf16[127,512]{1,0:T(8,128)(2,1)S(1)}, bf16[127,512]{1,0:T(8,128)(2,1)S(1)}, u32[]{:S(2)}, u32[]{:S(2)}) collective-permute-start(bf16[127,512]{1,0:T(8,128)(2,1)S(1)} %fusion.9), channel_id=1, source_target_pairs={{0,16},{16,32},{32,48},{48,64},{64,80},{80,96},{96,112},{112,128},... | collective-permute-start | bytes 390152 | tf_op jit(solution)/shard_map/ppermute | solution.py:13
where the time goes:
time: 136 us
  blocking collectives  102 us (75%)
  waiting for transfers between devices  10.8 us (8%)
  matrix products  9 us (7%)
  other arithmetic  5.95 us (4%)
  starting transfers between devices  4.17 us (3%)
  local copies, waits for them, and re-layouts  3.59 us (3%)
    all_gather x1, blocking collectives, on_device(): all_rows = lax.all_gather(edit_table, 'seq', axis=0, tiled=True)  56.8 us
    psum x1, blocking collectives, on_device(): summed = lax.psum(selected, 'chan')  45 us
    ppermute x2, waiting for transfers between devices, from_behind(): return lax.ppermute(block, axis, route)  10.8 us
    conv_general_dilated x2, matrix products, depth_conv(): lax.conv_general_dilated(window, kernel, (1,), 'VALID', dimension_numbers...  7.03 us
    ppermute x2, starting transfers between devices, from_behind(): return lax.ppermute(block, axis, route)  4.17 us
    convert_element_type x3, other arithmetic, on_device(): hidden = (second_gate.astype(jnp.float32) * long_out).astype(jnp.bfloat16)  3.39 us
  transfers between devices with their start and end apart: 2, of which 1 were waited for; matrix products, arithmetic and copies ran while one was open for 4% of the time, Pallas kernels for 0%

commit v1 on v0

--- a/solution.py
+++ b/solution.py
@@ -64,7 +64,9 @@
     hidden = (second_gate.astype(jnp.float32) * long_out).astype(jnp.bfloat16)
     rows_per = edit_table.shape[1]
     rank = rows_per // 2
-    all_rows = lax.all_gather(edit_table, "seq", axis=0, tiled=True)
+    all_rows = jnp.concatenate(
+        lax.all_to_all(jnp.stack([edit_table] * lax.axis_size("seq")), "seq", 0, 0), axis=0
+    )
     tenant_count = all_rows.shape[0]
     picker = (seq_tenant[:, None] == jnp.arange(tenant_count, dtype=jnp.int32)[None, :]).astype(
         jnp.bfloat16

time: 136 us -> 114 us (0.84)
  the two profiles are of different devices: /device:TPU:8 before, /device:TPU:24 now
where the time goes in v1:
time: 114 us
  blocking collectives  53.9 us (47%)
  starting transfers between devices  24.2 us (21%)
  waiting for transfers between devices  11.5 us (10%)
  matrix products  9.03 us (8%)
  local copies, waits for them, and re-layouts  7.86 us (7%)
  other arithmetic  6.82 us (6%)
    psum x1, blocking collectives, on_device(): summed = lax.psum(selected, 'chan')  53.9 us
    all_to_all x1, starting transfers between devices, on_device(): lax.all_to_all(jnp.stack([edit_table] * lax.axis_size('seq')), 'seq', 0, 0)  20.2 us
    ppermute x2, waiting for transfers between devices, from_behind(): return lax.ppermute(block, axis, route)  11.4 us
    conv_general_dilated x2, matrix products, depth_conv(): lax.conv_general_dilated(window, kernel, (1,), 'VALID', dimension_numbers...  7.06 us
    ppermute x2, starting transfers between devices, from_behind(): return lax.ppermute(block, axis, route)  3.94 us
    unnamed x33, local copies, waits for them, and re-layouts  2.71 us
    convert_element_type x3, other arithmetic, on_device(): hidden = (second_gate.astype(jnp.float32) * long_out).astype(jnp.bfloat16)  2.52 us
  transfers between devices with their start and end apart: 3, of which 1 were waited for; matrix products, arithmetic and copies ran while one was open for 16% of the time, Pallas kernels for 0%

profile of v1, /device:TPU:24, one launch (start us, length us, event | category | flops | bytes accessed | tf_op | source)
XLA Modules:
  0.0 113.5 jit_solution(4509380761886008372)
XLA Ops:
  0.0 1.2 %multiply_convert_fusion.3 = bf16[1,256,512]{2,1,0:T(8,128)(2,1)S(1)} fusion(bf16[5,256,512]{2,1,0:T(8,128)(2,1)} %param.7), kind=kLoop, calls=%fused_computation.15 | loop fusion | flops 524288 | bytes 786432 | tf_op jit(solution)/shard_map/convert_element_type | solution.py:57
  1.2 0.7 copy-done.4
  1.9 0.6 slice_bitcast_fusion
  2.5 1.9 %collective-permute-start = (bf16[6,512]{1,0:T(8,128)(2,1)}, bf16[6,512]{1,0:T(8,128)(2,1)}, u32[]{:S(2)}, u32[]{:S(2)}) collective-permute-start(bf16[6,512]{1,0:T(8,128)(2,1)} %slice_bitcast_fusion), channel_id=1, source_target_pairs={{0,16},{16,32},{32,48},{48,64},{64,80},{80,96},{96,112},{112,128},... | collective-permute-start | bytes 18440 | tf_op jit(solution)/shard_map/ppermute | solution.py:13
  4.4 1.6 %stack.2 = bf16[32,2,8,512]{3,2,1,0:T(8,128)(2,1)} broadcast(bf16[2,8,512]{2,1,0:T(8,128)(2,1)} %param.10), dimensions={1,2,3} | broadcast | bytes 540672 | tf_op jit(solution)/shard_map/stack | solution.py:68
  6.0 20.2 %all-to-all-start = ((bf16[32,2,8,512]{3,2,1,0:T(8,128)(2,1)}), bf16[32,2,8,512]{3,2,1,0:T(8,128)(2,1)S(1)}, u32[]{:S(2)}, u32[]{:S(2)}) async-start(bf16[32,2,8,512]{3,2,1,0:T(8,128)(2,1)} %stack.2), calls=%async_computation | async-start | bytes 1048576 | tf_op jit(solution)/shard_map/all_to_all | solution.py:68
  26.3 1.3 %slice_convert_fusion.2 = (f32[1,256,512]{2,1,0:T(8,128)S(1)}, f32[256,512]{1,0:T(8,128)}, f32[256,512]{1,0:T(8,128)}, f32[1,256,512]{2,1,0:T(8,128)S(1)}, f32[1,256,512]{2,1,0:T(8,128)S(1)}) fusion(bf16[5,256,512]{2,1,0:T(8,128)(2,1)S(1)} %copy-done.1), kind=kLoop, calls=%fused_computation.30 | loop fusion | flops 393216 | bytes 3407872 | tf_op jit(solution)/shard_map/convert_element_type | solution.py:64
  28.3 0.6 copy-done.10
  28.8 0.7 slice.59
  29.7 1.4 %rev.7 = bf16[128,512]{1,0:T(8,128)(2,1)} reverse(bf16[128,512]{1,0:T(8,128)(2,1)S(1)} %copy-done.5), dimensions={0} | reverse | bytes 262144 | tf_op jit(solution)/shard_map/rev | solution.py:18
  31.0 0.8 maximum_select_fusion.1
  31.8 1.0 pad_maximum_fusion.1
  33.1 0.2 pad.clone
  33.4 0.3 fusion.6
  33.7 0.3 convolution_select_fusion
  34.0 0.3 copy.54
  34.7 0.8 copy-done.2
  35.8 2.0 %collective-permute-start.1 = (bf16[127,512]{1,0:T(8,128)(2,1)S(1)}, bf16[127,512]{1,0:T(8,128)(2,1)S(1)}, u32[]{:S(2)}, u32[]{:S(2)}) collective-permute-start(bf16[127,512]{1,0:T(8,128)(2,1)S(1)} %fusion.9), channel_id=1, source_target_pairs={{0,16},{16,32},{32,48},{48,64},{64,80},{80,96},{96,112},{112,128},... | collective-permute-start | bytes 390152 | tf_op jit(solution)/shard_map/ppermute | solution.py:13
  38.0 11.4 %collective-permute-done.1 = bf16[127,512]{1,0:T(8,128)(2,1)S(1)} collective-permute-done((bf16[127,512]{1,0:T(8,128)(2,1)S(1)}, bf16[127,512]{1,0:T(8,128)(2,1)S(1)}, u32[]{:S(2)}, u32[]{:S(2)}) %collective-permute-start.1) | collective-permute-done | bytes 130080 | tf_op jit(solution)/shard_map/ppermute | solution.py:13
  49.7 6.7 %fusion.4 = f32[2,128,512]{2,0,1:T(2,128)S(1)} fusion(bf16[2,255,512]{2,1,0:T(8,128)(2,1)S(1)} %pad_maximum_fusion, bf16[128,1,512]{2,0,1:T(8,128)(2,1)S(1)} %bitcast.64), kind=kOutput, calls=%fused_computation.16 | convolution fusion | flops 33554432 | bytes 1177600 | tf_op jit(solution)/shard_map/conv_general_dilated | solution.py:19
  56.6 1.0 fusion.3
  57.8 0.2 convolution_convert_fusion
  58.3 53.9 %psum.7 = f32[256,8]{0,1:T(8,128)S(1)} all-reduce(f32[256,8]{0,1:T(8,128)S(1)} %fusion.2), channel_id=1, replica_groups=mesh['seq'=32,'chan'=16] {'chan'}, use_global_device_ids=true, to_apply=%region_4.5 | all-reduce | flops 2048 | bytes 16384 | tf_op jit(solution)/shard_map/psum | solution.py:87
  112.3 1.2 %fusion.1 = bf16[256,512]{1,0:T(8,128)(2,1)} fusion(bf16[256,512]{1,0:T(8,128)(2,1)S(1)} %fusion.3, bf16[4,8,512]{2,1,0:T(8,128)(2,1)S(1)} %bitcast.65, f32[256,4]{0,1:T(4,128)S(1)} %convolution_add_fusion, f32[256,4]{0,1:T(4,128)S(1)} %fusion.19), kind=kOutput, calls=%fused_computation.5 | convolution fusion | flops 25563136 | bytes 548864 | tf_op jit(solution)/shard_map/dot_general | solution.py:97
  (51 shorter events, 2.7 us)
Async XLA Ops:
  0.0 37.8 %copy-start = (f32[64,4]{0,1:T(4,128)S(1)}, f32[64,4]{0,1:T(4,128)}, u32[]{:S(2)}) copy-start(f32[64,4]{0,1:T(4,128)} %param.11) | copy-start | bytes 3076
  0.0 26.2 %copy-start.1 = (bf16[5,256,512]{2,1,0:T(8,128)(2,1)S(1)}, bf16[5,256,512]{2,1,0:T(8,128)(2,1)}, u32[]{:S(2)}) copy-start(bf16[5,256,512]{2,1,0:T(8,128)(2,1)} %param.7) | copy-start | bytes 3932164
  1.2 0.7 copy-start.4
  2.5 28.5 %collective-permute-start = (bf16[6,512]{1,0:T(8,128)(2,1)}, bf16[6,512]{1,0:T(8,128)(2,1)}, u32[]{:S(2)}, u32[]{:S(2)}) collective-permute-start(bf16[6,512]{1,0:T(8,128)(2,1)} %slice_bitcast_fusion), channel_id=1, source_target_pairs={{0,16},{16,32},{32,48},{48,64},{64,80},{80,96},{96,112},{112,128},... | collective-permute-start | bytes 18440 | tf_op jit(solution)/shard_map/ppermute | solution.py:13
  6.0 51.6 %all-to-all-start = ((bf16[32,2,8,512]{3,2,1,0:T(8,128)(2,1)}), bf16[32,2,8,512]{3,2,1,0:T(8,128)(2,1)S(1)}, u32[]{:S(2)}, u32[]{:S(2)}) async-start(bf16[32,2,8,512]{3,2,1,0:T(8,128)(2,1)} %stack.2), calls=%async_computation | async-start | bytes 1048576 | tf_op jit(solution)/shard_map/all_to_all | solution.py:68
  26.2 1.4 %copy-start.13 = (s32[4]{0:T(128)S(1)}, s32[4]{0:T(128)}, u32[]{:S(2)}) copy-start(s32[4]{0:T(128)} %param.12) | copy-start | bytes 52
  26.3 3.3 %copy-start.7 = (bf16[7,512]{1,0:T(8,128)(2,1)S(1)}, bf16[7,512]{1,0:T(8,128)(2,1)}, u32[]{:S(2)}) copy-start(bf16[7,512]{1,0:T(8,128)(2,1)} %param.8) | copy-start | bytes 21508
  26.3 3.4 %copy-start.5 = (bf16[128,512]{1,0:T(8,128)(2,1)S(1)}, bf16[128,512]{1,0:T(8,128)(2,1)}, u32[]{:S(2)}) copy-start(bf16[128,512]{1,0:T(8,128)(2,1)} %param.9) | copy-start | bytes 393220
  28.3 0.6 copy-start.10
  28.8 4.8 %copy-start.8 = (pred[2]{0:T(512)(128)(4,1)}, pred[2]{0:T(512)(128)(4,1)S(1)}, u32[]{:S(2)}) copy-start(pred[2]{0:T(512)(128)(4,1)S(1)} %compare_or_fusion) | copy-start | bytes 10
  31.0 2.7 %copy-start.14 = (pred[16,17]{0,1:T(8,128)(4,1)S(1)}, pred[16,17]{0,1:T(8,128)(4,1)}, u32[]{:S(2)}) copy-start(pred[16,17]{0,1:T(8,128)(4,1)} %constant.30) | copy-start | bytes 820
  34.5 1.0 copy-start.2
  34.5 1.2 %copy-start.3 = (f32[256,512]{1,0:T(8,128)S(1)}, f32[256,512]{1,0:T(8,128)}, u32[]{:S(2)}) copy-start(f32[256,512]{1,0:T(8,128)} %get-tuple-element.7) | copy-start | bytes 1572868
  34.5 3.3 %copy-start.12 = (s32[4]{0:T(128)S(1)}, s32[4]{0:T(128)}, u32[]{:S(2)}) copy-start(s32[4]{0:T(128)} %param.13) | copy-start | bytes 52
  34.5 15.0 %copy-start.9 = (pred[2]{0:T(512)(128)(4,1)S(1)}, pred[2]{0:T(512)(128)(4,1)}, u32[]{:S(2)}) copy-start(pred[2]{0:T(512)(128)(4,1)} %copy-done.8) | copy-start | bytes 10
  35.7 14.0 %copy-start.6 = (bf16[128,512]{1,0:T(8,128)(2,1)S(1)}, bf16[128,512]{1,0:T(8,128)(2,1)}, u32[]{:S(2)}) copy-start(bf16[128,512]{1,0:T(8,128)(2,1)} %rev.7) | copy-start | bytes 393220
  35.8 13.7 %collective-permute-start.1 = (bf16[127,512]{1,0:T(8,128)(2,1)S(1)}, bf16[127,512]{1,0:T(8,128)(2,1)S(1)}, u32[]{:S(2)}, u32[]{:S(2)}) collective-permute-start(bf16[127,512]{1,0:T(8,128)(2,1)S(1)} %fusion.9), channel_id=1, source_target_pairs={{0,16},{16,32},{32,48},{48,64},{64,80},{80,96},{96,112},{112,128},... | collective-permute-start | bytes 390152 | tf_op jit(solution)/shard_map/ppermute | solution.py:13
  56.6 55.6 %copy-start.11 = (s32[256]{0:T(256)S(1)}, s32[256]{0:T(256)}, u32[]{:S(2)}) copy-start(s32[256]{0:T(256)} %copy-done.10) | copy-start | bytes 3076
